TPU v7x, 32 devices: a whole 2x2x4 slice. The times are simulated.
32 devices in a mesh: groups: 2 (over y), dp: 4 (over z), tensor: 2 (over x), layer: 2 (over core).
Axes of the slice: x: 2, y: 2, z: 4, core: 2. Of those that a mesh axis runs over, the one named last changes fastest.
Arguments:
- hidden_in: bfloat16 [2, 8, 512, 14336], P('layer', ('groups', 'dp'), None, 'tensor'), parts along dimension 1, may hold values from -6 to 6
- out_grad: bfloat16 [2, 8, 512, 4096], P('layer', ('groups', 'dp'), 'tensor'), parts along dimension 1, may hold values from -6 to 6
- proj_in: bfloat16 [2, 14336, 64], P('layer', 'tensor'), may hold values from -0.046875 to 0.046875
- proj_out: bfloat16 [2, 4096, 64], P('layer'), may hold values from -0.09375 to 0.09375
- query_grads: bfloat16 [2, 1024, 4096], P('layer', 'dp', 'tensor'), may hold values from -1.5 to 1.5
- lengths: int32 [8], P(('groups', 'dp')), parts along dimension 0, may hold values from 128 to 512, as said below
- query_decision: int32 [1024], P('dp'), may hold values from 0 to 1023
Outputs:
- influence: float32 [8, 1024], P(('groups', 'dp')), parts along dimension 0
There are 2 independent parts, one for each index of `groups`. A program takes and returns all parts, laid end to end along the dimension named above; an argument that names none is the same for every part. Nothing has to cross between parts.
Inputs may be any that keep to these rules, and one draw needn't show every extreme that they name: `lengths`: in each part one transcript has all 512 tokens live and another has exactly 128.
All inputs are finite; a program needn't handle non-finite values.
Results may differ from a plain program's by a relative error of at most 0.004.
Values may be sent and summed in bfloat16 or wider, within the bound.
No kernel may reach another device: no remote copies, remote signals or barrier semaphores. Data moves between devices by JAX's collectives and lax.ppermute only.
A program may use at most 64 MiB of HBM per device.

v0:
```python
import jax
import jax.numpy as jnp
from jax import lax
from jax.sharding import PartitionSpec as P

DECISIONS = 1024


def body(hidden_in, out_grad, proj_in, proj_out, query_grads, lengths, query_decision):
    hidden_rows = hidden_in[0, 0]
    grad_rows = out_grad[0, 0]
    side_hidden = proj_in[0]
    side_width = proj_out[0]
    query_rows = query_grads[0]
    length = lengths[0]
    seq_shard = grad_rows.shape[0]
    first_pos = lax.axis_index("tensor") * seq_shard
    positions = first_pos + jnp.arange(seq_shard, dtype=jnp.int32)
    live = (positions < length).astype(jnp.float32)
    right = jnp.dot(grad_rows, side_width, preferred_element_type=jnp.float32)
    right = (right * live[:, None]).astype(jnp.bfloat16)
    right_full = lax.all_gather(right, "tensor", axis=0, tiled=True)
    left = jnp.dot(hidden_rows, side_hidden, preferred_element_type=jnp.float32)
    partial = jnp.dot(left.T, right_full.astype(jnp.float32), precision=lax.Precision.HIGHEST)
    partial = partial / length.astype(jnp.float32)
    grad_part = lax.psum_scatter(partial, "tensor", scatter_dimension=0, tiled=True)
    grad_flat = grad_part.reshape(1, -1).astype(jnp.bfloat16)
    grads_all = lax.all_gather(grad_flat, "dp", axis=0, tiled=True)
    scores = jnp.dot(grads_all, query_rows.T, preferred_element_type=jnp.float32)
    table = (query_decision[:, None] == jnp.arange(DECISIONS, dtype=jnp.int32)[None, :]).astype(
        jnp.float32
    )
    partial_dec = jnp.dot(scores, table, precision=lax.Precision.HIGHEST)
    total = lax.psum(partial_dec, ("dp", "tensor", "layer"))
    row = lax.dynamic_slice_in_dim(total, lax.axis_index("dp"), 1, axis=0)
    return row


def solution(mesh):
    in_specs = (
        P("layer", ("groups", "dp"), None, "tensor"),
        P("layer", ("groups", "dp"), "tensor", None),
        P("layer", "tensor", None),
        P("layer", None, None),
        P("layer", "dp", "tensor"),
        P(("groups", "dp")),
        P("dp"),
    )
    out_specs = P(("groups", "dp"), None)
    return jax.shard_map(body, mesh=mesh, in_specs=in_specs, out_specs=out_specs, check_vma=False)
```

profile of v0, /device:TPU:0, one launch (start us, length us, event | category | flops | bytes accessed | tf_op | source)
XLA Modules:
  0.0 113.7 jit_solution(15606715019655168779)
XLA Ops:
  6.5 0.0 copy-start
  6.5 0.0 copy-start.1
  6.5 0.0 copy-start.2
  6.5 0.0 reduce-scatter.2.cloned.1.call-start
  7.4 0.8 copy-done
  8.1 1.8 %fusion.7 = bf16[256,64]{0,1:T(8,128)(2,1)S(1)} fusion(bf16[1,1,256,4096]{3,2,1,0:T(8,128)(2,1)S(1)} %copy-done, bf16[1,4096,64]{1,2,0:T(8,128)(2,1)} %param.10, f32[256]{0:T(256)S(1)} %compare_convert_fusion), kind=kOutput, calls=%fused_computation.5 | convolution fusion | flops 134250496 | bytes 2655232 | tf_op jit(solution)/shard_map/dot_general | solution.py:20
  9.9 5.5 %all_gather.6 = bf16[512,64]{0,1:T(8,128)(2,1)S(1)} all-gather(bf16[256,64]{0,1:T(8,128)(2,1)S(1)} %fusion.7), channel_id=1, replica_groups=mesh['groups'=2,'dp'=4,'tensor'=2,'layer'=2] {'tensor'}, dimensions={0}, use_global_device_ids=true | all-gather | bytes 98304 | tf_op jit(solution)/shard_map/all_gather | solution.py:22
  15.5 5.6 %fusion = f32[512,64]{0,1:T(8,128)S(1)} fusion(bf16[1,1,512,7168]{3,2,1,0:T(8,128)(2,1)} %param.7, bf16[1,7168,64]{1,2,0:T(8,128)(2,1)} %param.9), kind=kOutput, calls=%fused_computation | convolution fusion | flops 469762048 | bytes 8388608 | tf_op jit(solution)/shard_map/dot_general | solution.py:23
  21.1 0.8 convolution_divide_fusion
  21.9 0.0 reduce-scatter.2.cloned.1.call-update
  21.9 11.9 %reduce-scatter.2.cloned.1.call-done = f32[32,64]{1,0:T(8,128)} async-done(((f32[64,64]{1,0:T(8,128)}), f32[32,64]{1,0:T(8,128)}) %reduce-scatter.2.cloned.1.call-update) | async-done | bytes 8208 | tf_op jit(solution)/shard_map/reduce_scatter | solution.py:26
  33.8 0.7 convert_element_type.32
  34.5 0.1 reshape.21
  34.6 13.2 %all-gather = bf16[4,1,2048]{2,1,0:T(2,128)(2,1)S(1)} all-gather(bf16[1,1,2048]{2,1,0:T(2,128)(2,1)S(1)} %reshape.21), channel_id=1, replica_groups=mesh['groups'=2,'dp'=4,'tensor'=2,'layer'=2] {'dp'}, dimensions={0}, use_global_device_ids=true | all-gather | bytes 20480 | tf_op jit(solution)/shard_map/all_gather | solution.py:28
  47.8 0.0 copy-done.1
  47.8 0.4 fusion.10
  48.2 0.0 copy-done.2
  48.2 0.5 fusion.12
  48.7 57.6 %psum.7 = f32[4,1024]{1,0:T(4,128)S(1)} all-reduce(f32[4,1024]{1,0:T(4,128)S(1)} %fusion.12), channel_id=1, replica_groups=mesh['groups'=2,'dp'=4,'tensor'=2,'layer'=2] {'dp','tensor','layer'}, use_global_device_ids=true, to_apply=%region_1.0 | all-reduce | flops 4096 | bytes 32768 | tf_op jit(solution)/shard_map/psum | solution.py:34
  106.3 0.6 constant_dynamic-slice_fusion
  (1 shorter events, 0.0 us)
Async XLA Ops:
  6.5 1.6 %copy-start = (bf16[1,1,256,4096]{3,2,1,0:T(8,128)(2,1)S(1)}, bf16[1,1,256,4096]{3,2,1,0:T(8,128)(2,1)}, u32[]{:S(2)}) copy-start(bf16[1,1,256,4096]{3,2,1,0:T(8,128)(2,1)} %param.8) | copy-start | bytes 6291460
  6.5 41.2 %copy-start.1 = (bf16[1,256,2048]{2,1,0:T(8,128)(2,1)S(1)}, bf16[1,256,2048]{2,1,0:T(8,128)(2,1)}, u32[]{:S(2)}) copy-start(bf16[1,256,2048]{2,1,0:T(8,128)(2,1)} %param.11) | copy-start | bytes 3145732
  6.5 41.6 %copy-start.2 = (s32[256]{0:T(256)S(1)}, s32[256]{0:T(256)}, u32[]{:S(2)}) copy-start(s32[256]{0:T(256)} %param.13) | copy-start | bytes 3076
  6.5 27.3 %reduce-scatter.2.cloned.1.call-start = ((), (), s32[]{:S(2)}) async-start(), calls=%async_computation.1 | async-start | bytes 49152 | tf_op jit(solution)/shard_map/reduce_scatter | solution.py:26
Sparse Core Ops, SparseCore 0:
  22.0 11.7 reduce-scatter.1
where the time goes:
time: 114 us
  blocking collectives  76.3 us (67%)
  between operations  14.2 us (12%)
  waiting for transfers between devices  11.9 us (10%)
  matrix products  9.12 us (8%)
  local copies, waits for them, and re-layouts  1.48 us (1%)
    psum x1, blocking collectives, body(): total = lax.psum(partial_dec, ('dp', 'tensor', 'layer'))  57.6 us
    all_gather x1, blocking collectives, body(): grads_all = lax.all_gather(grad_flat, 'dp', axis=0, tiled=True)  13.2 us
    reduce_scatter x1, waiting for transfers between devices, body(): lax.psum_scatter(partial, 'tensor', scatter_dimension=0, tiled=True)  11.9 us
    dot_general x1, matrix products, body(): left = jnp.dot(hidden_rows, side_hidden, preferred_element_type=jnp.float32)  5.61 us
    all_gather x1, blocking collectives, body(): right_full = lax.all_gather(right, 'tensor', axis=0, tiled=True)  5.51 us
  transfers between devices with their start and end apart: 1, of which 1 were waited for; matrix products, arithmetic and copies ran while one was open for 0% of the time, Pallas kernels for 0%

commit v1 on v0

--- a/solution.py
+++ b/solution.py
@@ -25,7 +25,15 @@
     partial = partial / length.astype(jnp.float32)
     grad_part = lax.psum_scatter(partial, "tensor", scatter_dimension=0, tiled=True)
     grad_flat = grad_part.reshape(1, -1).astype(jnp.bfloat16)
-    grads_all = lax.all_gather(grad_flat, "dp", axis=0, tiled=True)
+    ways, here = (lax.axis_size("dp"), lax.axis_index("dp"))
+    grown, reach = (grad_flat, 1)
+    while reach < ways:
+        theirs = lax.ppermute(grown, "dp", [(d, d ^ reach) for d in range(ways)])
+        mine_first = jnp.concatenate([grown, theirs], axis=0)
+        theirs_first = jnp.concatenate([theirs, grown], axis=0)
+        grown = jnp.where(here & reach == 0, mine_first, theirs_first)
+        reach = 2 * reach
+    grads_all = grown
     scores = jnp.dot(grads_all, query_rows.T, preferred_element_type=jnp.float32)
     table = (query_decision[:, None] == jnp.arange(DECISIONS, dtype=jnp.int32)[None, :]).astype(
         jnp.float32

time: 114 us -> 109 us (0.956)
  blocking collectives: 76.3 us -> 63.5 us
  waiting for transfers between devices: 11.9 us -> 16.2 us
  starting transfers between devices: 0.01 us -> 3.96 us
    all_gather x1 -> x0, blocking collectives: 13.2 us -> none  [body(): grads_all = lax.all_gather(grad_flat, 'dp', axis=0, tiled=True)]
    ppermute x0 -> x2, waiting for transfers between devices: none -> 4.31 us  [body(): theirs = lax.ppermute(grown, 'dp', [(d, d ^ reach) for d in range(ways)])]
    ppermute x0 -> x2, starting transfers between devices: none -> 3.96 us  [body(): theirs = lax.ppermute(grown, 'dp', [(d, d ^ reach) for d in range(ways)])]
  transfers between devices with their start and end apart: 1 -> 3, of which waited for: 1 -> 3; matrix products, arithmetic and copies ran while one was open for 0% -> 0% of each run, Pallas kernels for 0% -> 0%
where the time goes in v1:
time: 109 us
  blocking collectives  63.5 us (58%)
  waiting for transfers between devices  16.2 us (15%)
  between operations  14.2 us (13%)
  matrix products  8.91 us (8%)
  starting transfers between devices  3.96 us (4%)
  local copies, waits for them, and re-layouts  1.48 us (1%)
    psum x1, blocking collectives, body(): total = lax.psum(partial_dec, ('dp', 'tensor', 'layer'))  57.6 us
    reduce_scatter x1, waiting for transfers between devices, body(): lax.psum_scatter(partial, 'tensor', scatter_dimension=0, tiled=True)  11.9 us
    all_gather x1, blocking collectives, body(): right_full = lax.all_gather(right, 'tensor', axis=0, tiled=True)  5.86 us
    dot_general x1, matrix products, body(): left = jnp.dot(hidden_rows, side_hidden, preferred_element_type=jnp.float32)  5.3 us
    ppermute x2, waiting for transfers between devices, body(): theirs = lax.ppermute(grown, 'dp', [(d, d ^ reach) for d in range(ways)])  4.31 us
    ppermute x2, starting transfers between devices, body(): theirs = lax.ppermute(grown, 'dp', [(d, d ^ reach) for d in range(ways)])  3.96 us
  transfers between devices with their start and end apart: 3, of which 3 were waited for; matrix products, arithmetic and copies ran while one was open for 0% of the time, Pallas kernels for 0%

profile of v1, /device:TPU:0, one launch (start us, length us, event | category | flops | bytes accessed | tf_op | source)
XLA Modules:
  0.0 109.1 jit_solution(2589841993983319861)
XLA Ops:
  6.5 0.0 copy-start
  6.5 0.0 copy-start.1
  6.5 0.0 copy-start.2
  6.5 0.0 reduce-scatter.2.cloned.1.call-start
  7.4 0.8 copy-done
  8.1 1.7 %fusion.7 = bf16[256,64]{1,0:T(8,128)(2,1)S(1)} fusion(bf16[1,1,256,4096]{3,2,1,0:T(8,128)(2,1)S(1)} %copy-done, bf16[1,4096,64]{1,2,0:T(8,128)(2,1)} %param.10, f32[256]{0:T(256)S(1)} %compare_convert_fusion), kind=kOutput, calls=%fused_computation.5 | convolution fusion | flops 134250496 | bytes 2655232 | tf_op jit(solution)/shard_map/dot_general | solution.py:20
  9.9 5.9 %all_gather.3 = bf16[512,64]{1,0:T(8,128)(2,1)S(1)} all-gather(bf16[256,64]{1,0:T(8,128)(2,1)S(1)} %fusion.7), channel_id=1, replica_groups=mesh['groups'=2,'dp'=4,'tensor'=2,'layer'=2] {'tensor'}, dimensions={0}, use_global_device_ids=true | all-gather | bytes 98304 | tf_op jit(solution)/shard_map/all_gather | solution.py:22
  15.7 5.3 %fusion = f32[512,64]{1,0:T(8,128)S(1)} fusion(bf16[1,1,512,7168]{3,2,1,0:T(8,128)(2,1)} %param.7, bf16[1,7168,64]{1,2,0:T(8,128)(2,1)} %param.9), kind=kOutput, calls=%fused_computation | convolution fusion | flops 469762048 | bytes 8388608 | tf_op jit(solution)/shard_map/dot_general | solution.py:23
  21.1 1.0 convolution_divide_fusion
  22.0 0.0 reduce-scatter.2.cloned.1.call-update
  22.1 11.9 %reduce-scatter.2.cloned.1.call-done = f32[32,64]{1,0:T(8,128)} async-done(((f32[64,64]{1,0:T(8,128)}), f32[32,64]{1,0:T(8,128)}) %reduce-scatter.2.cloned.1.call-update) | async-done | bytes 8208 | tf_op jit(solution)/shard_map/reduce_scatter | solution.py:26
  34.0 0.7 convert_element_type.32
  34.7 0.1 convert_element_type.33
  34.8 1.5 %collective-permute-start = (bf16[1,2048]{1,0:T(2,128)(2,1)S(1)}, bf16[1,2048]{1,0:T(2,128)(2,1)S(1)}, u32[]{:S(2)}, u32[]{:S(2)}) collective-permute-start(bf16[1,2048]{1,0:T(2,128)(2,1)S(1)} %convert_element_type.33), channel_id=1, source_target_pairs={{0,4},{4,0},{8,12},{12,8},{1,5},{5,1},{9,13},{13,9},{2,6},{6,2},{1... | collective-permute-start | bytes 12296 | tf_op jit(solution)/shard_map/ppermute | solution.py:31
  36.3 2.2 %collective-permute-done = bf16[1,2048]{1,0:T(2,128)(2,1)S(1)} collective-permute-done((bf16[1,2048]{1,0:T(2,128)(2,1)S(1)}, bf16[1,2048]{1,0:T(2,128)(2,1)S(1)}, u32[]{:S(2)}, u32[]{:S(2)}) %collective-permute-start) | collective-permute-done | bytes 4128 | tf_op jit(solution)/shard_map/ppermute | solution.py:31
  38.5 2.5 %collective-permute-start.1 = (bf16[2,2048]{1,0:T(2,128)(2,1)S(1)}, bf16[2,2048]{1,0:T(2,128)(2,1)S(1)}, u32[]{:S(2)}, u32[]{:S(2)}) collective-permute-start(bf16[2,2048]{1,0:T(2,128)(2,1)S(1)} %broadcast_select_fusion), channel_id=1, source_target_pairs={{0,8},{4,12},{8,0},{12,4},{1,9},{5,13},{9,1},{13,5},{2,10},{6,14},... | collective-permute-start | bytes 24584 | tf_op jit(solution)/shard_map/ppermute | solution.py:31
  41.0 2.1 %collective-permute-done.1 = bf16[2,2048]{1,0:T(2,128)(2,1)S(1)} collective-permute-done((bf16[2,2048]{1,0:T(2,128)(2,1)S(1)}, bf16[2,2048]{1,0:T(2,128)(2,1)S(1)}, u32[]{:S(2)}, u32[]{:S(2)}) %collective-permute-start.1) | collective-permute-done | bytes 8224 | tf_op jit(solution)/shard_map/ppermute | solution.py:31
  43.1 0.0 copy-done.1
  43.1 0.4 fusion.10
  43.5 0.0 copy-done.2
  43.5 0.5 fusion.12
  44.0 57.6 %psum.7 = f32[4,1024]{1,0:T(4,128)S(1)} all-reduce(f32[4,1024]{1,0:T(4,128)S(1)} %fusion.12), channel_id=1, replica_groups=mesh['groups'=2,'dp'=4,'tensor'=2,'layer'=2] {'dp','tensor','layer'}, use_global_device_ids=true, to_apply=%region_1.2 | all-reduce | flops 4096 | bytes 32768 | tf_op jit(solution)/shard_map/psum | solution.py:42
  101.6 0.6 constant_dynamic-slice_fusion
  (2 shorter events, 0.0 us)
Async XLA Ops:
  6.5 1.6 %copy-start = (bf16[1,1,256,4096]{3,2,1,0:T(8,128)(2,1)S(1)}, bf16[1,1,256,4096]{3,2,1,0:T(8,128)(2,1)}, u32[]{:S(2)}) copy-start(bf16[1,1,256,4096]{3,2,1,0:T(8,128)(2,1)} %param.8) | copy-start | bytes 6291460
  6.5 36.6 %copy-start.1 = (bf16[1,256,2048]{2,1,0:T(8,128)(2,1)S(1)}, bf16[1,256,2048]{2,1,0:T(8,128)(2,1)}, u32[]{:S(2)}) copy-start(bf16[1,256,2048]{2,1,0:T(8,128)(2,1)} %param.11) | copy-start | bytes 3145732
  6.5 36.9 %copy-start.2 = (s32[256]{0:T(256)S(1)}, s32[256]{0:T(256)}, u32[]{:S(2)}) copy-start(s32[256]{0:T(256)} %param.13) | copy-start | bytes 3076
  6.5 27.4 %reduce-scatter.2.cloned.1.call-start = ((), (), s32[]{:S(2)}) async-start(), calls=%async_computation.1 | async-start | bytes 49152 | tf_op jit(solution)/shard_map/reduce_scatter | solution.py:26
  34.8 3.7 %collective-permute-start = (bf16[1,2048]{1,0:T(2,128)(2,1)S(1)}, bf16[1,2048]{1,0:T(2,128)(2,1)S(1)}, u32[]{:S(2)}, u32[]{:S(2)}) collective-permute-start(bf16[1,2048]{1,0:T(2,128)(2,1)S(1)} %convert_element_type.33), channel_id=1, source_target_pairs={{0,4},{4,0},{8,12},{12,8},{1,5},{5,1},{9,13},{13,9},{2,6},{6,2},{1... | collective-permute-start | bytes 12296 | tf_op jit(solution)/shard_map/ppermute | solution.py:31
  38.5 4.6 %collective-permute-start.1 = (bf16[2,2048]{1,0:T(2,128)(2,1)S(1)}, bf16[2,2048]{1,0:T(2,128)(2,1)S(1)}, u32[]{:S(2)}, u32[]{:S(2)}) collective-permute-start(bf16[2,2048]{1,0:T(2,128)(2,1)S(1)} %broadcast_select_fusion), channel_id=1, source_target_pairs={{0,8},{4,12},{8,0},{12,4},{1,9},{5,13},{9,1},{13,5},{2,10},{6,14},... | collective-permute-start | bytes 24584 | tf_op jit(solution)/shard_map/ppermute | solution.py:31
Sparse Core Ops, SparseCore 0:
  22.2 11.7 reduce-scatter.1

commit v2 on v0

--- a/solution.py
+++ b/solution.py
@@ -31,7 +31,7 @@
         jnp.float32
     )
     partial_dec = jnp.dot(scores, table, precision=lax.Precision.HIGHEST)
-    total = lax.psum(partial_dec, ("dp", "tensor", "layer"))
+    total = jnp.sum(lax.all_gather(partial_dec, ("dp", "tensor", "layer")), axis=0)
     row = lax.dynamic_slice_in_dim(total, lax.axis_index("dp"), 1, axis=0)
     return row
 

time: 114 us -> 77.5 us (0.68)
  blocking collectives: 76.3 us -> 39.7 us
    psum x1 -> x0, blocking collectives: 57.6 us -> none  [body(): total = lax.psum(partial_dec, ('dp', 'tensor', 'layer'))]
    all_gather x0 -> x1, blocking collectives: none -> 21.1 us  [body(): lax.all_gather(partial_dec, ('dp', 'tensor', 'layer'))]
where the time goes in v2:
time: 77.5 us; the launch traced here: 77.3 us
  blocking collectives  39.7 us (51%)
  between operations  14.2 us (18%)
  waiting for transfers between devices  11.9 us (15%)
  matrix products  9.12 us (12%)
  local copies, waits for them, and re-layouts  1.48 us (2%)
  other arithmetic  0.78 us (1%)
    all_gather x1, blocking collectives, body(): lax.all_gather(partial_dec, ('dp', 'tensor', 'layer'))  21.1 us
    all_gather x1, blocking collectives, body(): grads_all = lax.all_gather(grad_flat, 'dp', axis=0, tiled=True)  13.2 us
    reduce_scatter x1, waiting for transfers between devices, body(): lax.psum_scatter(partial, 'tensor', scatter_dimension=0, tiled=True)  11.9 us
    dot_general x1, matrix products, body(): left = jnp.dot(hidden_rows, side_hidden, preferred_element_type=jnp.float32)  5.61 us
    all_gather x1, blocking collectives, body(): right_full = lax.all_gather(right, 'tensor', axis=0, tiled=True)  5.51 us
    dot_general x1, matrix products, body(): right = jnp.dot(grad_rows, side_width, preferred_element_type=jnp.float32)  1.8 us
  transfers between devices with their start and end apart: 1, of which 1 were waited for; matrix products, arithmetic and copies ran while one was open for 0% of the time, Pallas kernels for 0%

profile of v2, /device:TPU:0, one launch (start us, length us, event | category | flops | bytes accessed | tf_op | source)
XLA Modules:
  0.0 77.3 jit_solution(7835386923562751296)
XLA Ops:
  6.5 0.0 copy-start
  6.5 0.0 copy-start.1
  6.5 0.0 copy-start.2
  6.5 0.0 reduce-scatter.2.cloned.1.call-start
  7.4 0.8 %copy-done = bf16[1,1,256,4096]{3,2,1,0:T(8,128)(2,1)S(1)} copy-done((bf16[1,1,256,4096]{3,2,1,0:T(8,128)(2,1)S(1)}, bf16[1,1,256,4096]{3,2,1,0:T(8,128)(2,1)}, u32[]{:S(2)}) %copy-start) | copy-done | bytes 2097176
  8.1 1.8 %fusion.7 = bf16[256,64]{0,1:T(8,128)(2,1)S(1)} fusion(bf16[1,1,256,4096]{3,2,1,0:T(8,128)(2,1)S(1)} %copy-done, bf16[1,4096,64]{1,2,0:T(8,128)(2,1)} %param.10, f32[256]{0:T(256)S(1)} %compare_convert_fusion), kind=kOutput, calls=%fused_computation.5 | convolution fusion | flops 134250496 | bytes 2655232 | tf_op jit(solution)/shard_map/dot_general | solution.py:20
  9.9 5.5 %all_gather.12 = bf16[512,64]{0,1:T(8,128)(2,1)S(1)} all-gather(bf16[256,64]{0,1:T(8,128)(2,1)S(1)} %fusion.7), channel_id=1, replica_groups=mesh['groups'=2,'dp'=4,'tensor'=2,'layer'=2] {'tensor'}, dimensions={0}, use_global_device_ids=true | all-gather | bytes 98304 | tf_op jit(solution)/shard_map/all_gather | solution.py:22
  15.5 5.6 %fusion = f32[512,64]{0,1:T(8,128)S(1)} fusion(bf16[1,1,512,7168]{3,2,1,0:T(8,128)(2,1)} %param.7, bf16[1,7168,64]{1,2,0:T(8,128)(2,1)} %param.9), kind=kOutput, calls=%fused_computation | convolution fusion | flops 469762048 | bytes 8388608 | tf_op jit(solution)/shard_map/dot_general | solution.py:23
  21.1 0.8 %convolution_divide_fusion = f32[64,64]{1,0:T(8,128)} fusion(f32[512,64]{0,1:T(8,128)S(1)} %fusion, bf16[512,64]{0,1:T(8,128)(2,1)S(1)} %all_gather.12, f32[]{:T(128)S(6)} %convert_element_type.31), kind=kOutput, calls=%fused_computation.6 | convolution fusion | flops 25169920 | bytes 212996 | tf_op jit(solution)/shard_map/dot_general | solution.py:24
  21.9 0.0 reduce-scatter.2.cloned.1.call-update
  21.9 11.9 %reduce-scatter.2.cloned.1.call-done = f32[32,64]{1,0:T(8,128)} async-done(((f32[64,64]{1,0:T(8,128)}), f32[32,64]{1,0:T(8,128)}) %reduce-scatter.2.cloned.1.call-update) | async-done | bytes 8208 | tf_op jit(solution)/shard_map/reduce_scatter | solution.py:26
  33.8 0.7 convert_element_type.32
  34.5 0.1 reshape.22
  34.6 13.2 %all-gather.1 = bf16[4,1,2048]{2,1,0:T(2,128)(2,1)S(1)} all-gather(bf16[1,1,2048]{2,1,0:T(2,128)(2,1)S(1)} %reshape.22), channel_id=1, replica_groups=mesh['groups'=2,'dp'=4,'tensor'=2,'layer'=2] {'dp'}, dimensions={0}, use_global_device_ids=true | all-gather | bytes 20480 | tf_op jit(solution)/shard_map/all_gather | solution.py:28
  47.8 0.0 copy-done.1
  47.8 0.4 fusion.10
  48.2 0.0 copy-done.2
  48.2 0.5 convolution_bitcast_fusion
  48.7 21.1 %all-gather.2 = f32[16,4,1024]{2,1,0:T(4,128)S(1)} all-gather(f32[1,4,1024]{2,1,0:T(4,128)S(1)} %convolution_bitcast_fusion), channel_id=2, replica_groups=mesh['groups'=2,'dp'=4,'tensor'=2,'layer'=2] {'dp','tensor','layer'}, dimensions={0}, use_global_device_ids=true | all-gather | bytes 278528 | tf_op jit(solution)/shard_map/all_gather | solution.py:34
  69.8 0.1 reduce_sum.9
  69.8 0.6 constant_dynamic-slice_fusion
  (1 shorter events, 0.0 us)
Async XLA Ops:
  6.5 1.6 %copy-start = (bf16[1,1,256,4096]{3,2,1,0:T(8,128)(2,1)S(1)}, bf16[1,1,256,4096]{3,2,1,0:T(8,128)(2,1)}, u32[]{:S(2)}) copy-start(bf16[1,1,256,4096]{3,2,1,0:T(8,128)(2,1)} %param.8) | copy-start | bytes 6291460
  6.5 41.2 %copy-start.1 = (bf16[1,256,2048]{2,1,0:T(8,128)(2,1)S(1)}, bf16[1,256,2048]{2,1,0:T(8,128)(2,1)}, u32[]{:S(2)}) copy-start(bf16[1,256,2048]{2,1,0:T(8,128)(2,1)} %param.11) | copy-start | bytes 3145732
  6.5 41.6 %copy-start.2 = (s32[256]{0:T(256)S(1)}, s32[256]{0:T(256)}, u32[]{:S(2)}) copy-start(s32[256]{0:T(256)} %param.13) | copy-start | bytes 3076
  6.5 27.3 %reduce-scatter.2.cloned.1.call-start = ((), (), s32[]{:S(2)}) async-start(), calls=%async_computation.1 | async-start | bytes 49152 | tf_op jit(solution)/shard_map/reduce_scatter | solution.py:26
Sparse Core Ops, SparseCore 0:
  22.0 11.7 reduce-scatter.1
